TPU v7x, 32 devices: a whole 2x2x4 slice. The times are simulated.
32 devices in a mesh: group: 2 (over x), gx: 16 (over z, y, core).
Axes of the slice: x: 2, y: 2, z: 4, core: 2. Of those that a mesh axis runs over, the one named last changes fastest.
Arguments:
- fields: float32 [128, 256, 256], P(('group', 'gx')), parts along dimension 0, may hold values from -6 to 6
- courant: float32 [128, 16384], P(('group', 'gx')), parts along dimension 0, may hold values from -0.8 to 0.8
- switches: int32 [2, 128, 16384], P(None, ('group', 'gx')), parts along dimension 1, may hold values 0 or 1
- strip_table: int32 [512], P('group'), parts along dimension 0, may hold values from 0 to 15, never falling along the last dimension, each value on 1 to 32 neighbouring positions
- weight_in: bfloat16 [2304, 256], replicated, may hold values from -0.125 to 0.125
- bias_in: float32 [256], replicated, may hold values from -3 to 3
- weight_mid: bfloat16 [16, 256, 256], P('gx'), may hold values from -0.375 to 0.375
- bias_mid: float32 [16, 256], P('gx'), may hold values from -3 to 3
- weight_out: bfloat16 [16, 256, 256], P('gx'), may hold values from -0.375 to 0.375
- bias_out: float32 [16, 256], P('gx'), may hold values from -3 to 3
Outputs:
- fields_next: float32 [128, 256, 256], P(('group', 'gx')), parts along dimension 0
There are 2 independent parts, one for each index of `group`. A program takes and returns all parts, laid end to end along the dimension named above; an argument that names none is the same for every part. Nothing has to cross between parts.
Inputs may be any that keep to these rules, and one draw needn't show every extreme that they name: `strip_table`: never falls along the rows; every band holds 1 to 32 consecutive rows, and some band exactly 32.
All inputs are finite; a program needn't handle non-finite values. No bound on the sum of `switches` on one device may be relied on, other than what follows from the above.
Results may differ from a plain program's by a relative error of at most 0.0028.
Values may be sent and summed in bfloat16 or wider, within the bound.
No kernel may reach another device: no remote copies, remote signals or barrier semaphores. Data moves between devices by JAX's collectives and lax.ppermute only.
A program may use at most 64 MiB of HBM per device.

v0:
```python
import jax
import jax.numpy as jnp
from jax import lax
from jax.sharding import PartitionSpec as P


def as_sent(array):
    return jax.tree.map(lambda a: a.astype(jnp.bfloat16) if a.dtype == jnp.float32 else a, array)


def passed_along(array, axis, by):
    length = lax.axis_size(axis)
    return lax.ppermute(array, axis, [(i, (i + by) % length) for i in range(length)])


def padded_2(cells, sides, width):
    for axis, dim in sides:
        count = lax.axis_size(axis)
        head = lax.slice_in_dim(cells, 0, width, axis=dim)
        tail = lax.slice_in_dim(cells, cells.shape[dim] - width, cells.shape[dim], axis=dim)
        cells = jnp.concatenate(
            [
                lax.ppermute(tail, axis, [(i, (i + 1) % count) for i in range(count)]),
                cells,
                lax.ppermute(head, axis, [((i + 1) % count, i) for i in range(count)]),
            ],
            axis=dim,
        )
    return cells


def lead_of(values):
    return passed_along(as_sent(values[:1]), "gx", -1)


def face_flux(left_vals, right_vals, speeds, switch_now):
    damping = switch_now * speeds * speeds + (1.0 - switch_now) * jnp.abs(speeds)
    return 0.5 * speeds * (left_vals + right_vals) - 0.5 * damping * (right_vals - left_vals)


def flux_change(values, right_col, speeds, switch_now):
    right_vals = jnp.concatenate([values[1:], right_col], 0)
    edge_flux = face_flux(values, right_vals, speeds, switch_now)
    left_flux = passed_along(as_sent(edge_flux[-1:]), "gx", 1)
    return edge_flux - jnp.concatenate([left_flux, edge_flux[:-1]], 0)


def first_layer(slot_data, weight_in, bias_in, lon_dev, tile_rows):
    slot_count = slot_data.shape[0]
    channels = slot_data.shape[-1]
    hidden = weight_in.shape[1]
    weights = weight_in.reshape(3, 3, channels, hidden)
    summed = jnp.zeros((slot_count * lon_dev * tile_rows, hidden), jnp.float32)
    for lon_off in range(3):
        for lat_off in range(3):
            window = slot_data[
                :, lon_off : lon_off + lon_dev, lat_off : lat_off + tile_rows, :
            ].reshape(-1, channels)
            summed = summed + jnp.dot(
                window, weights[lon_off, lat_off], preferred_element_type=jnp.float32
            )
    hidden_one = jax.nn.silu(summed + bias_in).astype(jnp.bfloat16)
    return hidden_one.reshape(slot_count, lon_dev, tile_rows, hidden)


def on_device(
    fields,
    courant,
    switches,
    strip_table,
    weight_in,
    bias_in,
    weight_mid,
    bias_mid,
    weight_out,
    bias_out,
):
    lon_dev, lat_rows, channels = fields.shape
    levels = courant.shape[1] // lat_rows
    field_count = channels // levels
    devices = lax.axis_size("gx")
    tiles_dev = strip_table.shape[0]
    tile_rows = lat_rows // tiles_dev
    capacity = max(2, 2 * tiles_dev // devices)
    speeds = courant.reshape(lon_dev, lat_rows, 1, levels)
    onehot = (strip_table[:, None] == jnp.arange(devices, dtype=jnp.int32)[None, :]).astype(
        jnp.int32
    )
    before = jnp.cumsum(onehot, 0) - onehot
    slot_rank = jnp.sum(before * onehot, 1)
    slot_index = strip_table * capacity + slot_rank
    current = fields
    columns_bf = padded_2(current.astype(jnp.bfloat16), (("gx", 0),), 1)
    padded = jnp.pad(columns_bf, ((0, 0), (1, 1), (0, 0)))
    tile_data = jnp.stack(
        [padded[:, offset : offset + lat_rows : tile_rows] for offset in range(tile_rows + 2)], 2
    )
    tile_data = tile_data.transpose(1, 0, 2, 3)
    holder = jnp.zeros((devices * capacity,) + tile_data.shape[1:], tile_data.dtype)
    holder = holder.at[slot_index].set(tile_data)
    received = lax.all_to_all(
        holder.reshape((devices, capacity) + tile_data.shape[1:]),
        "gx",
        split_axis=0,
        concat_axis=0,
        tiled=True,
    )
    sources = received.shape[0]
    slots = received.shape[1]
    flat_slots = received.reshape((sources * slots,) + received.shape[2:])
    hidden_one = first_layer(flat_slots, weight_in, bias_in, lon_dev, tile_rows)
    finish_hidden_one = hidden_one.reshape((sources, slots) + hidden_one.shape[1:])
    leading = finish_hidden_one.shape[:-1]
    row_block = finish_hidden_one.reshape(-1, finish_hidden_one.shape[-1])
    middle = jnp.dot(row_block, weight_mid[0], preferred_element_type=jnp.float32)
    hidden_two = jax.nn.silu(middle + bias_mid[0]).astype(jnp.bfloat16)
    result = jnp.dot(hidden_two, weight_out[0], preferred_element_type=jnp.float32) + bias_out[0]
    tendency = result.astype(jnp.bfloat16).reshape(leading + (channels,))
    returned = lax.all_to_all(tendency, "gx", split_axis=0, concat_axis=0, tiled=True)
    tendency = returned.reshape((devices * capacity,) + returned.shape[2:])[slot_index]
    tendency = tendency.transpose(1, 0, 2, 3).reshape(lon_dev, lat_rows, channels)
    layered = current.reshape(lon_dev, lat_rows, field_count, levels)
    switch_one = switches[0].reshape(lon_dev, lat_rows, 1, levels).astype(jnp.float32)
    switch_two = switches[1].reshape(lon_dev, lat_rows, 1, levels).astype(jnp.float32)
    ahead_col = lead_of(current).reshape(1, lat_rows, field_count, levels)
    section_one = layered - flux_change(layered, ahead_col, speeds, switch_one)
    ahead_two = lead_of(section_one)
    section_two = section_one - flux_change(section_one, ahead_two, speeds, switch_two)
    moved = 0.5 * layered + 0.5 * section_two
    current = moved.reshape(lon_dev, lat_rows, channels) + tendency.astype(jnp.float32)
    return current


def solution(mesh):
    return jax.shard_map(
        on_device,
        mesh=mesh,
        in_specs=(
            P(("group", "gx"), None, None),
            P(("group", "gx"), None),
            P(None, ("group", "gx"), None),
            P("group"),
            P(),
            P(),
            P("gx", None, None),
            P("gx", None),
            P("gx", None, None),
            P("gx", None),
        ),
        out_specs=P(("group", "gx"), None, None),
        check_vma=False,
    )
```

profile of v0, /device:TPU:0, one launch (start us, length us, event | category | flops | bytes accessed | tf_op | source)
XLA Modules:
  0.0 286.5 jit_solution(11881718784824937256)
XLA Ops:
  2.0 5.5 %collective-permute-start.5 = (bf16[1,256,256]{2,1,0:T(8,128)(2,1)}, bf16[1,256,256]{2,1,0:T(8,128)(2,1)S(1)}, u32[]{:S(2)}, u32[]{:S(2)}) collective-permute-start(bf16[1,256,256]{2,1,0:T(8,128)(2,1)} %get-tuple-element.19), channel_id=1, source_target_pairs={{1,0},{2,1},{3,2},{4,3},{5,4},{6,5},{7,6},{8,7},{9,8},{10,9},{11,1... | collective-permute-start | bytes 393224 | tf_op jit(solution)/shard_map/ppermute | solution.py:25
  10.3 4.3 %collective-permute-done.4 = bf16[1,256,256]{2,1,0:T(8,128)(2,1)S(1)} collective-permute-done((bf16[1,256,256]{2,1,0:T(8,128)(2,1)S(1)}, bf16[1,256,256]{2,1,0:T(8,128)(2,1)S(1)}, u32[]{:S(2)}, u32[]{:S(2)}) %collective-permute-start.4) | collective-permute-done | bytes 131104 | tf_op jit(solution)/shard_map/ppermute | solution.py:23
  16.7 3.0 %broadcast_in_dim.4 = bf16[512,6,3,256]{3,1,2,0:T(8,128)(2,1)} broadcast(bf16[]{:T(256)} %constant.8.clone.1), dimensions={} | broadcast | bytes 4718594 | tf_op jit(solution)/shard_map/broadcast_in_dim | solution.py:99
  19.7 29.4 %scatter_fusion = bf16[512,6,3,256]{3,1,2,0:T(8,128)(2,1)} fusion(bf16[512,6,3,256]{3,1,2,0:T(8,128)(2,1)} %broadcast_in_dim.4, s32[256]{0:T(256)S(1)} %compare_select_fusion, bf16[256,6,3,256]{3,1,2,0:T(8,128)(2,1)S(1)} %copy.125), kind=kCustom, calls=%fused_computation.1 | custom fusion | bytes 7078912 | tf_op jit(solution)/shard_map/scatter | solution.py:100
  49.1 6.4 %copy.126 = bf16[16,32,6,3,256]{4,1,3,2,0:T(8,128)(2,1)} copy(bf16[16,32,6,3,256]{4,2,3,1,0:T(8,128)(2,1)} %bitcast.119) | data formatting | bytes 9437184 | tf_op jit(solution)/shard_map/reshape | solution.py:102
  55.5 4.6 %all-to-all-start = ((bf16[16,32,6,3,256]{4,1,3,2,0:T(8,128)(2,1)}), bf16[16,32,6,3,256]{4,1,3,2,0:T(8,128)(2,1)}, u32[]{:S(2)}, u32[]{:S(2)}) async-start(bf16[16,32,6,3,256]{4,1,3,2,0:T(8,128)(2,1)} %copy.126), calls=%async_computation | async-start | bytes 9437184 | tf_op jit(solution)/shard_map/all_to_all | solution.py:101
  60.1 4.3 %collective-permute-start = (bf16[1,256,256]{2,1,0:T(8,128)(2,1)}, bf16[1,256,256]{2,1,0:T(8,128)(2,1)}, u32[]{:S(2)}, u32[]{:S(2)}) collective-permute-start(bf16[1,256,256]{2,1,0:T(8,128)(2,1)} %get-tuple-element.19), channel_id=1, source_target_pairs={{0,15},{1,0},{2,1},{3,2},{4,3},{5,4},{6,5},{7,6},{8,7},{9,8},{10,9... | collective-permute-start | bytes 393224 | tf_op jit(solution)/shard_map/ppermute | solution.py:13
  64.4 82.3 %all-to-all-done = bf16[16,32,6,3,256]{4,1,3,2,0:T(8,128)(2,1)} async-done(((bf16[16,32,6,3,256]{4,1,3,2,0:T(8,128)(2,1)}), bf16[16,32,6,3,256]{4,1,3,2,0:T(8,128)(2,1)}, u32[]{:S(2)}, u32[]{:S(2)}) %all-to-all-start) | async-done | bytes 4718624 | tf_op jit(solution)/shard_map/all_to_all | solution.py:101
  146.7 2.9 %copy.127 = bf16[16,32,6,3,256]{4,1,0,3,2:T(8,128)(2,1)S(1)} copy(bf16[16,32,6,3,256]{4,1,3,2,0:T(8,128)(2,1)} %all-to-all-done) | data formatting | bytes 9437184 | tf_op jit(solution)/shard_map/all_to_all | solution.py:101
  149.6 2.7 fusion.24
  155.5 3.0 %copy.129 = bf16[512,4,1,256]{3,1,0,2:T(4,128)(2,1)} copy(bf16[512,4,1,256]{3,0,2,1:T(8,128)(2,1)} %get-tuple-element.12) | data formatting | bytes 2097152 | tf_op jit(solution)/shard_map/slice | solution.py:56
  160.7 3.0 %copy.130 = bf16[512,4,1,256]{3,1,0,2:T(4,128)(2,1)} copy(bf16[512,4,1,256]{3,0,2,1:T(8,128)(2,1)} %get-tuple-element.11) | data formatting | bytes 2097152 | tf_op jit(solution)/shard_map/slice | solution.py:56
  165.9 3.0 %copy.131 = bf16[512,4,1,256]{3,1,0,2:T(4,128)(2,1)} copy(bf16[512,4,1,256]{3,0,2,1:T(8,128)(2,1)} %get-tuple-element.10) | data formatting | bytes 2097152 | tf_op jit(solution)/shard_map/slice | solution.py:56
  171.1 3.0 %copy.132 = bf16[512,4,1,256]{3,1,0,2:T(4,128)(2,1)} copy(bf16[512,4,1,256]{3,0,2,1:T(8,128)(2,1)} %get-tuple-element.9) | data formatting | bytes 2097152 | tf_op jit(solution)/shard_map/slice | solution.py:56
  176.2 3.0 %copy.133 = bf16[512,4,1,256]{3,1,0,2:T(4,128)(2,1)} copy(bf16[512,4,1,256]{3,0,2,1:T(8,128)(2,1)} %get-tuple-element.8) | data formatting | bytes 2097152 | tf_op jit(solution)/shard_map/slice | solution.py:56
  181.4 3.0 %copy.134 = bf16[512,4,1,256]{3,1,0,2:T(4,128)(2,1)} copy(bf16[512,4,1,256]{3,0,2,1:T(8,128)(2,1)} %get-tuple-element.7) | data formatting | bytes 2097152 | tf_op jit(solution)/shard_map/slice | solution.py:56
  204.4 23.2 %all-to-all-start.1 = ((bf16[16,32,4,1,256]{4,2,1,3,0:T(4,128)(2,1)}), bf16[16,32,4,1,256]{4,2,1,3,0:T(4,128)(2,1)}, u32[]{:S(2)}, u32[]{:S(2)}) async-start(bf16[16,32,4,1,256]{4,2,1,3,0:T(4,128)(2,1)} %bitcast.34), calls=%async_computation.1 | async-start | bytes 2097152 | tf_op jit(solution)/shard_map/all_to_all | solution.py:119
  235.2 16.6 %collective-permute-done.1 = bf16[1,256,4,64]{1,3,2,0:T(8,128)(2,1)S(1)} collective-permute-done((bf16[1,256,4,64]{1,3,2,0:T(8,128)(2,1)S(1)}, bf16[1,256,4,64]{1,3,2,0:T(8,128)(2,1)S(1)}, u32[]{:S(2)}, u32[]{:S(2)}) %collective-permute-start.1) | collective-permute-done | bytes 131104 | tf_op jit(solution)/shard_map/ppermute | solution.py:13
  252.6 2.5 collective-permute-done.2
  257.1 2.6 copy.102
  260.8 2.5 copy.108
  265.5 2.6 copy.121
  280.0 2.4 gather_fusion
  282.5 4.1 %fusion.7 = f32[4,256,256]{2,1,0:T(8,128)} fusion(f32[4,256,256]{2,1,0:T(8,128)S(1)} %copy-done.1, f32[3,256,256]{2,1,0:T(8,128)} %copy.123, f32[1,256,256]{2,1,0:T(8,128)} %copy.122, f32[4,256,256]{2,1,0:T(8,128)} %copy.121, f32[4,256,256]{2,1,0:T(8,128)S(1)} %copy-done.6, f32[3,256,256]{2,1,0:T(8,128)} %copy.113, f32[1,256,256]{2,1,0:T(8,128)} %copy.112, ...), kind=kLoop, calls=%fused_computation.29 | loop fusion | flops 5767168 | bytes 9961472 | tf_op jit(solution)/shard_map/add | solution.py:130
  (137 shorter events, 66.3 us)
Async XLA Ops:
  0.0 202.2 %copy-start = (bf16[1,256,256]{2,1,0:T(8,128)(2,1)S(1)}, bf16[1,256,256]{2,1,0:T(8,128)(2,1)}, u32[]{:S(2)}) copy-start(bf16[1,256,256]{2,1,0:T(8,128)(2,1)} %param.18) | copy-start | bytes 393220
  0.0 7.5 %copy-start.24 = (s32[256]{0:T(256)S(1)}, s32[256]{0:T(256)}, u32[]{:S(2)}) copy-start(s32[256]{0:T(256)} %param.13) | copy-start | bytes 3076
  2.0 8.3 %collective-permute-start.5 = (bf16[1,256,256]{2,1,0:T(8,128)(2,1)}, bf16[1,256,256]{2,1,0:T(8,128)(2,1)S(1)}, u32[]{:S(2)}, u32[]{:S(2)}) collective-permute-start(bf16[1,256,256]{2,1,0:T(8,128)(2,1)} %get-tuple-element.19), channel_id=1, source_target_pairs={{1,0},{2,1},{3,2},{4,3},{5,4},{6,5},{7,6},{8,7},{9,8},{10,9},{11,1... | collective-permute-start | bytes 393224 | tf_op jit(solution)/shard_map/ppermute | solution.py:25
  7.5 7.1 %collective-permute-start.4 = (bf16[1,256,256]{2,1,0:T(8,128)(2,1)S(1)}, bf16[1,256,256]{2,1,0:T(8,128)(2,1)S(1)}, u32[]{:S(2)}, u32[]{:S(2)}) collective-permute-start(bf16[1,256,256]{2,1,0:T(8,128)(2,1)S(1)} %get-tuple-element.18), channel_id=1, source_target_pairs={{0,1},{1,2},{2,3},{3,4},{4,5},{5,6},{6,7},{7,8},{8,9},{9,10},{10,1... | collective-permute-start | bytes 393224 | tf_op jit(solution)/shard_map/ppermute | solution.py:23
  55.5 91.2 %all-to-all-start = ((bf16[16,32,6,3,256]{4,1,3,2,0:T(8,128)(2,1)}), bf16[16,32,6,3,256]{4,1,3,2,0:T(8,128)(2,1)}, u32[]{:S(2)}, u32[]{:S(2)}) async-start(bf16[16,32,6,3,256]{4,1,3,2,0:T(8,128)(2,1)} %copy.126), calls=%async_computation | async-start | bytes 9437184 | tf_op jit(solution)/shard_map/all_to_all | solution.py:101
  60.1 171.4 %collective-permute-start = (bf16[1,256,256]{2,1,0:T(8,128)(2,1)}, bf16[1,256,256]{2,1,0:T(8,128)(2,1)}, u32[]{:S(2)}, u32[]{:S(2)}) collective-permute-start(bf16[1,256,256]{2,1,0:T(8,128)(2,1)} %get-tuple-element.19), channel_id=1, source_target_pairs={{0,15},{1,0},{2,1},{3,2},{4,3},{5,4},{6,5},{7,6},{8,7},{9,8},{10,9... | collective-permute-start | bytes 393224 | tf_op jit(solution)/shard_map/ppermute | solution.py:13
  191.8 1.6 copy-start.21
  203.2 24.3 %copy-start.22 = (s32[2,4,16384]{2,1,0:T(4,128)S(1)}, s32[2,4,16384]{2,1,0:T(4,128)}, u32[]{:S(2)}) copy-start(s32[2,4,16384]{2,1,0:T(4,128)} %param.12) | copy-start | bytes 1572868
  204.4 75.7 %all-to-all-start.1 = ((bf16[16,32,4,1,256]{4,2,1,3,0:T(4,128)(2,1)}), bf16[16,32,4,1,256]{4,2,1,3,0:T(4,128)(2,1)}, u32[]{:S(2)}, u32[]{:S(2)}) async-start(bf16[16,32,4,1,256]{4,2,1,3,0:T(4,128)(2,1)} %bitcast.34), calls=%async_computation.1 | async-start | bytes 2097152 | tf_op jit(solution)/shard_map/all_to_all | solution.py:119
  228.4 1.5 copy-start.1
  230.0 3.3 %copy-start.4 = (f32[4,256,64]{1,2,0:T(8,128)}, f32[4,256,64]{1,2,0:T(8,128)S(1)}, u32[]{:S(2)}) copy-start(f32[4,256,64]{1,2,0:T(8,128)S(1)} %get-tuple-element.24) | copy-start | bytes 786436
  230.0 25.2 %copy-start.15 = (f32[4,256,64]{1,2,0:T(8,128)}, f32[4,256,64]{1,2,0:T(8,128)S(1)}, u32[]{:S(2)}) copy-start(f32[4,256,64]{1,2,0:T(8,128)S(1)} %get-tuple-element.22) | copy-start | bytes 786436
  234.7 17.0 %collective-permute-start.1 = (bf16[1,256,4,64]{1,3,2,0:T(8,128)(2,1)S(1)}, bf16[1,256,4,64]{1,3,2,0:T(8,128)(2,1)S(1)}, u32[]{:S(2)}, u32[]{:S(2)}) collective-permute-start(bf16[1,256,4,64]{1,3,2,0:T(8,128)(2,1)S(1)} %slice.199), channel_id=1, source_target_pairs={{0,1},{1,2},{2,3},{3,4},{4,5},{5,6},{6,7},{7,8},{8,9},{9,10},{10,1... | collective-permute-start | bytes 393224 | tf_op jit(solution)/shard_map/ppermute | solution.py:13
  235.2 16.8 %copy-start.2 = (f32[3,256,4,64]{1,3,2,0:T(8,128)}, f32[3,256,4,64]{1,3,2,0:T(8,128)S(1)}, u32[]{:S(2)}) copy-start(f32[3,256,4,64]{1,3,2,0:T(8,128)S(1)} %slice.146) | copy-start | bytes 2359300
  252.5 2.6 copy-start.5
  252.5 2.6 collective-permute-start.2
  255.1 2.0 copy-start.17
  255.4 1.8 copy-start.14
  255.4 4.3 %copy-start.16 = (f32[4,256,64]{1,2,0:T(8,128)S(1)}, f32[4,256,64]{1,2,0:T(8,128)}, u32[]{:S(2)}) copy-start(f32[4,256,64]{1,2,0:T(8,128)} %get-tuple-element.23) | copy-start | bytes 786436
  256.1 22.2 %collective-permute-start.3 = (bf16[1,256,4,64]{1,3,2,0:T(8,128)(2,1)}, bf16[1,256,4,64]{1,3,2,0:T(8,128)(2,1)}, u32[]{:S(2)}, u32[]{:S(2)}) collective-permute-start(bf16[1,256,4,64]{1,3,2,0:T(8,128)(2,1)} %slice.197), channel_id=1, source_target_pairs={{0,1},{1,2},{2,3},{3,4},{4,5},{5,6},{6,7},{7,8},{8,9},{9,10},{10,1... | collective-permute-start | bytes 393224 | tf_op jit(solution)/shard_map/ppermute | solution.py:13
  263.3 4.7 %copy-start.3 = (f32[3,256,4,64]{1,3,2,0:T(8,128)S(1)}, f32[3,256,4,64]{1,3,2,0:T(8,128)}, u32[]{:S(2)}) copy-start(f32[3,256,4,64]{1,3,2,0:T(8,128)} %copy-done.2) | copy-start | bytes 2359300
  269.2 2.9 %copy-start.20 = (f32[1,256,4,64]{1,3,2,0:T(8,128)S(1)}, f32[1,256,4,64]{1,3,2,0:T(8,128)}, u32[]{:S(2)}) copy-start(f32[1,256,4,64]{1,3,2,0:T(8,128)} %copy-done.19) | copy-start | bytes 786436
  272.1 5.4 %copy-start.18 = (f32[1,256,4,64]{1,3,2,0:T(8,128)S(1)}, f32[1,256,4,64]{1,3,2,0:T(8,128)}, u32[]{:S(2)}) copy-start(f32[1,256,4,64]{1,3,2,0:T(8,128)} %copy-done.17) | copy-start | bytes 786436
  275.1 7.4 %copy-start.6 = (f32[4,256,256]{2,1,0:T(8,128)S(1)}, f32[4,256,256]{2,1,0:T(8,128)}, u32[]{:S(2)}) copy-start(f32[4,256,256]{2,1,0:T(8,128)} %copy.102) | copy-start | bytes 3145732
  (13 other events, 14.0 us)
where the time goes:
time: 292 us; the launch traced here: 287 us
  local copies, waits for them, and re-layouts  123 us (42%)
  waiting for transfers between devices  108 us (37%)
  starting transfers between devices  37.9 us (13%)
  other arithmetic  12 us (4%)
  matrix products  6.06 us (2%)
    all_to_all x1, waiting for transfers between devices, on_device(): lax.all_to_all(holder.reshape((devices, capacity) + tile_data.shape[1:]),...  82.3 us
    scatter x1, local copies, waits for them, and re-layouts, on_device(): holder = holder.at[slot_index].set(tile_data)  29.4 us
    slice x10, local copies, waits for them, and re-layouts, first_layer(): slot_data[:, lon_off:lon_off + lon_dev, lat_off:lat_off + tile_rows, :]  25.3 us
    all_to_all x1, starting transfers between devices, on_device(): lax.all_to_all(tendency, 'gx', split_axis=0, concat_axis=0, tiled=True)  23.2 us
    ppermute x4, waiting for transfers between devices, passed_along(): lax.ppermute(array, axis, [(i, (i + by) % length) for i in range(length)])  19 us
    reshape x9, local copies, waits for them, and re-layouts, first_layer(): window = slot_data[:, lon_off:lon_off + lon_dev, lat_off:lat_off + tile_r...  16.9 us
    mul x4, local copies, waits for them, and re-layouts, face_flux(): 0.5 * damping * (right_vals - left_vals)  8.34 us
    reshape x1, local copies, waits for them, and re-layouts, on_device(): holder.reshape((devices, capacity) + tile_data.shape[1:])  6.41 us
  transfers between devices with their start and end apart: 8, of which 5 were waited for; matrix products, arithmetic and copies ran while one was open for 30% of the time, Pallas kernels for 0%

commit v1 on v0

v1 whole, which is shorter than its diff:
```python
import functools

import jax
import jax.numpy as jnp
from jax import lax
from jax.experimental import pallas as pl
from jax.experimental.pallas import tpu as pltpu
from jax.sharding import PartitionSpec as P


def passed_along(array, axis, by):
    length = lax.axis_size(axis)
    return lax.ppermute(array, axis, [(i, (i + by) % length) for i in range(length)])


def face_flux(left_vals, right_vals, speeds, switch_now):
    damping = switch_now * speeds * speeds + (1.0 - switch_now) * jnp.abs(speeds)
    return 0.5 * speeds * (left_vals + right_vals) - 0.5 * damping * (right_vals - left_vals)


def flux_change(values, right_col, speeds, switch_now):
    right_vals = jnp.concatenate([values[1:], right_col], 0)
    edge_flux = face_flux(values, right_vals, speeds, switch_now)
    left_flux = passed_along(edge_flux[-1:].astype(jnp.bfloat16), "gx", 1).astype(jnp.float32)
    return edge_flux - jnp.concatenate([left_flux, edge_flux[:-1]], 0)


def band_kernel(tile_ref, band_ref, valid_ref, h1_ref, bid_ref, wm_ref, bm_ref, wo_ref, bo_ref, out_ref):
    step = pl.program_id(0)
    band = band_ref[step]
    first = jnp.logical_or(step == 0, tile_ref[step] != tile_ref[jnp.maximum(step - 1, 0)])

    @pl.when(first)
    def _():
        out_ref[...] = jnp.zeros_like(out_ref)

    @pl.when(valid_ref[step] == 1)
    def _():
        lon, rows, hidden = h1_ref.shape
        block = h1_ref[...].reshape(lon * rows, hidden)
        middle = jnp.dot(block, wm_ref[0], preferred_element_type=jnp.float32) + bm_ref[0]
        hidden_two = (middle / (1.0 + jnp.exp(-middle))).astype(jnp.bfloat16)
        result = jnp.dot(hidden_two, wo_ref[0], preferred_element_type=jnp.float32) + bo_ref[0]
        result = result.astype(jnp.bfloat16).astype(jnp.float32)
        result = result.reshape(lon, rows, result.shape[-1])
        mask = (bid_ref[...] == band)[None]
        out_ref[...] = jnp.where(mask, result, out_ref[...])


def band_networks(hidden_one, strip_table, weight_mid, bias_mid, weight_out, bias_out, tile_rows):
    lon, lat_rows, hidden = hidden_one.shape
    channels = weight_out.shape[-1]
    bands = weight_mid.shape[0]
    tiles = lat_rows // tile_rows
    steps = tiles + bands - 1
    low = strip_table[0::tile_rows]
    high = strip_table[tile_rows - 1 :: tile_rows]
    count = high - low + 1
    offset = jnp.cumsum(count) - count
    total = jnp.sum(count)
    index = jnp.arange(steps, dtype=jnp.int32)
    tile = jnp.clip(jnp.searchsorted(offset, index, side="right").astype(jnp.int32) - 1, 0, tiles - 1)
    band = low[tile] + (index - offset[tile])
    valid = index < total
    tile = jnp.where(valid, tile, tiles - 1).astype(jnp.int32)
    band = jnp.clip(jnp.where(valid, band, high[tiles - 1]), 0, bands - 1).astype(jnp.int32)
    valid = valid.astype(jnp.int32)
    band_ids = strip_table.reshape(lat_rows, 1)
    grid_spec = pltpu.PrefetchScalarGridSpec(
        num_scalar_prefetch=3,
        grid=(steps,),
        in_specs=[
            pl.BlockSpec((lon, tile_rows, hidden), lambda s, t, b, v: (0, t[s], 0)),
            pl.BlockSpec((tile_rows, 1), lambda s, t, b, v: (t[s], 0)),
            pl.BlockSpec((1, hidden, hidden), lambda s, t, b, v: (b[s], 0, 0)),
            pl.BlockSpec((1, 1, hidden), lambda s, t, b, v: (b[s], 0, 0)),
            pl.BlockSpec((1, hidden, channels), lambda s, t, b, v: (b[s], 0, 0)),
            pl.BlockSpec((1, 1, channels), lambda s, t, b, v: (b[s], 0, 0)),
        ],
        out_specs=pl.BlockSpec((lon, tile_rows, channels), lambda s, t, b, v: (0, t[s], 0)),
    )
    return pl.pallas_call(
        band_kernel,
        grid_spec=grid_spec,
        out_shape=jax.ShapeDtypeStruct((lon, lat_rows, channels), jnp.float32),
        compiler_params=pltpu.CompilerParams(dimension_semantics=("arbitrary",)),
    )(
        tile,
        band,
        valid,
        hidden_one,
        band_ids,
        weight_mid,
        bias_mid.reshape(bands, 1, hidden),
        weight_out,
        bias_out.reshape(bands, 1, channels),
    )


def on_device(
    fields,
    courant,
    switches,
    strip_table,
    weight_in,
    bias_in,
    weight_mid,
    bias_mid,
    weight_out,
    bias_out,
):
    lon_dev, lat_rows, channels = fields.shape
    levels = courant.shape[1] // lat_rows
    field_count = channels // levels
    hidden = weight_in.shape[1]
    tile_rows = min(32, lat_rows)

    all_mid = lax.all_gather(weight_mid, "gx", axis=0, tiled=True)
    all_bmid = lax.all_gather(bias_mid, "gx", axis=0, tiled=True)
    all_out = lax.all_gather(weight_out, "gx", axis=0, tiled=True)
    all_bout = lax.all_gather(bias_out, "gx", axis=0, tiled=True)

    columns_bf = fields.astype(jnp.bfloat16)
    west_col = passed_along(columns_bf[-1:], "gx", 1)
    east_col = passed_along(columns_bf[:1], "gx", -1)
    padded = jnp.concatenate([west_col, columns_bf, east_col], 0)
    padded = jnp.pad(padded, ((0, 0), (1, 1), (0, 0)))
    kernel = weight_in.reshape(3, 3, channels, hidden)
    summed = lax.conv_general_dilated(
        padded[None],
        kernel,
        (1, 1),
        "VALID",
        dimension_numbers=("NHWC", "HWIO", "NHWC"),
        preferred_element_type=jnp.float32,
    )[0]
    summed = summed + bias_in
    hidden_one = jax.nn.silu(summed).astype(jnp.bfloat16)

    tendency = band_networks(hidden_one, strip_table, all_mid, all_bmid, all_out, all_bout, tile_rows)

    speeds = courant.reshape(lon_dev, lat_rows, 1, levels)
    layered = fields.reshape(lon_dev, lat_rows, field_count, levels)
    switch_one = switches[0].reshape(lon_dev, lat_rows, 1, levels).astype(jnp.float32)
    switch_two = switches[1].reshape(lon_dev, lat_rows, 1, levels).astype(jnp.float32)
    ahead_col = east_col.astype(jnp.float32).reshape(1, lat_rows, field_count, levels)
    section_one = layered - flux_change(layered, ahead_col, speeds, switch_one)
    ahead_two = passed_along(section_one[:1].astype(jnp.bfloat16), "gx", -1).astype(jnp.float32)
    section_two = section_one - flux_change(section_one, ahead_two, speeds, switch_two)
    moved = 0.5 * layered + 0.5 * section_two
    return moved.reshape(lon_dev, lat_rows, channels) + tendency


def solution(mesh):
    return jax.shard_map(
        on_device,
        mesh=mesh,
        in_specs=(
            P(("group", "gx"), None, None),
            P(("group", "gx"), None),
            P(None, ("group", "gx"), None),
            P("group"),
            P(),
            P(),
            P("gx", None, None),
            P("gx", None),
            P("gx", None, None),
            P("gx", None),
        ),
        out_specs=P(("group", "gx"), None, None),
        check_vma=False,
    )
```

time: 292 us -> 147 us (0.50); the launches traced: 287 us -> 145 us
  waiting for transfers between devices: 108 us -> 6.75 us
  local copies, waits for them, and re-layouts: 123 us -> 37.3 us
  blocking collectives: 0 us -> 38.9 us
  starting transfers between devices: 37.9 us -> 6.62 us
  Pallas kernels: 0 us -> 16.3 us
  between operations: 0.42 us -> 13.7 us
  other arithmetic: 12 us -> 18.5 us
    all_to_all x2 -> x0, waiting for transfers between devices: 82.3 us -> none  [the longest x1 82.3 us: on_device(): lax.all_to_all(holder.reshape((devices, capacity) + tile_data.shape[1:]),...]
    all_gather x0 -> x2, blocking collectives: none -> 38.9 us  [the longest x1 20.6 us: on_device(): all_bmid = lax.all_gather(bias_mid, 'gx', axis=0, tiled=True)]
    scatter x1 -> x0, local copies, waits for them, and re-layouts: 29.4 us -> none  [on_device(): holder = holder.at[slot_index].set(tile_data)]
    all_to_all x2 -> x0, starting transfers between devices: 27.7 us -> none  [the longest x1 23.2 us: on_device(): lax.all_to_all(tendency, 'gx', split_axis=0, concat_axis=0, tiled=True)]
    slice x15 -> x7, local copies, waits for them, and re-layouts: 26.8 us -> 2.18 us  [the longest x1 0.71 us: on_device(): west_col = passed_along(columns_bf[-1:], 'gx', 1)]
    reshape x11 -> x1, local copies, waits for them, and re-layouts: 24.4 us -> 0.8 us  [band_networks(): band_ids = strip_table.reshape(lat_rows, 1)]
    pallas_call x0 -> x1, Pallas kernels: none -> 16.3 us  [band_networks(): pl.pallas_call(band_kernel, grid_spec=grid_spec, out_shape=jax.ShapeDtype...]
    ppermute x4 -> x5, waiting for transfers between devices: 19 us -> 6.02 us  [passed_along(): lax.ppermute(array, axis, [(i, (i + by) % length) for i in range(length)])]
  transfers between devices with their start and end apart: 8 -> 7, of which waited for: 5 -> 1; matrix products, arithmetic and copies ran while one was open for 30% -> 38% of each run, Pallas kernels for 0% -> 0%
where the time goes in v1:
time: 147 us; the launch traced here: 145 us
  blocking collectives  38.9 us (26%)
  local copies, waits for them, and re-layouts  37.3 us (25%)
  other arithmetic  18.5 us (13%)
  Pallas kernels  16.3 us (11%)
  between operations  13.7 us (9%)
  matrix products  6.89 us (5%)
  waiting for transfers between devices  6.75 us (5%)
  starting transfers between devices  6.62 us (5%)
    all_gather x1, blocking collectives, on_device(): all_bmid = lax.all_gather(bias_mid, 'gx', axis=0, tiled=True)  20.6 us
    all_gather x1, blocking collectives, on_device(): all_bout = lax.all_gather(bias_out, 'gx', axis=0, tiled=True)  18.3 us
    pallas_call x1, Pallas kernels, band_networks(): pl.pallas_call(band_kernel, grid_spec=grid_spec, out_shape=jax.ShapeDtype...  16.3 us
    mul x4, local copies, waits for them, and re-layouts, face_flux(): 0.5 * damping * (right_vals - left_vals)  9.16 us
    conv_general_dilated x1, matrix products, on_device(): lax.conv_general_dilated(padded[None], kernel, (1, 1), 'VALID', dimension...  6.89 us
    ppermute x5, starting transfers between devices, passed_along(): lax.ppermute(array, axis, [(i, (i + by) % length) for i in range(length)])  6.58 us
    ppermute x5, waiting for transfers between devices, passed_along(): lax.ppermute(array, axis, [(i, (i + by) % length) for i in range(length)])  6.02 us
    add x1, other arithmetic, on_device(): return moved.reshape(lon_dev, lat_rows, channels) + tendency  4.63 us
  transfers between devices with their start and end apart: 7, of which 1 were waited for; matrix products, arithmetic and copies ran while one was open for 38% of the time, Pallas kernels for 0%

profile of v1, /device:TPU:0, one launch (start us, length us, event | category | flops | bytes accessed | tf_op | source)
XLA Modules:
  0.0 145.1 jit_solution(2978161474623216570)
XLA Ops:
  7.3 1.3 convert_element_type.56
  10.6 5.0 %collective-permute-start = (bf16[1,256,256]{2,1,0:T(8,128)(2,1)}, bf16[1,256,256]{2,1,0:T(8,128)(2,1)}, u32[]{:S(2)}, u32[]{:S(2)}) collective-permute-start(bf16[1,256,256]{2,1,0:T(8,128)(2,1)} %get-tuple-element.101), channel_id=1, source_target_pairs={{0,15},{1,0},{2,1},{3,2},{4,3},{5,4},{6,5},{7,6},{8,7},{9,8},{10,9... | collective-permute-start | bytes 393224 | tf_op jit(solution)/shard_map/ppermute | solution.py:13
  16.7 3.0 %while.24 = (s32[]{:T(128)}, u32[23]{0:T(128)S(1)}, u32[23]{0:T(128)S(1)}, s32[8]{0:T(128)S(1)}, s32[]{:T(128)}, /*index=5*/s32[]{:T(128)}, s32[]{}) while((s32[]{:T(128)}, u32[23]{0:T(128)S(1)}, u32[23]{0:T(128)S(1)}, s32[8]{0:T(128)S(1)}, s32[]{:T(128)}, /*index=5*/s32[]{:T(128)}, s32[]{}) %tuple.39), condition=%wide.region_3.4_spmd.clone, body=%wide.region_2.3_spmd.clone.sunk | while | flops 1327 | bytes 5300 | solution.py:62
  25.2 1.7 %select_clamp_fusion.band_ref = s32[23]{0:T(128)} fusion(s32[23]{0:T(128)S(1)} %gather_fusion.1, s32[23]{0:T(128)S(1)} %gather_fusion.2, s32[]{:T(128)} %bitcast.14, s32[]{:T(128)} %get-tuple-element.106), kind=kLoop, calls=%fused_computation.55 | loop fusion | flops 115 | bytes 284 | tf_op jit(solution)/shard_map/jit(clip)/min | solution.py:66
  29.0 2.4 %copy.57 = f32[3,256,256]{1,2,0:T(8,128)} copy(f32[3,256,256]{2,1,0:T(8,128)} %slice.48) | data formatting | bytes 1572864 | tf_op jit(solution)/shard_map/slice | solution.py:22
  31.4 2.0 %mul.147 = f32[4,256,4,64]{1,3,2,0:T(8,128)} broadcast(f32[4,256,64]{1,2,0:T(8,128)} %get-tuple-element.102), dimensions={0,1,3} | broadcast | bytes 1310720 | tf_op jit(solution)/shard_map/mul | solution.py:18
  33.5 2.6 %copy.68 = f32[4,256,256]{2,1,0:T(8,128)} copy(f32[4,256,256]{1,2,0:T(8,128)} %bitcast.35) | data formatting | bytes 2097152 | tf_op jit(solution)/shard_map/mul | solution.py:18
  36.1 2.0 %mul.137 = f32[4,256,4,64]{1,3,2,0:T(8,128)} broadcast(f32[4,256,64]{1,2,0:T(8,128)} %get-tuple-element.103), dimensions={0,1,3} | broadcast | bytes 1310720 | tf_op jit(solution)/shard_map/mul | solution.py:18
  38.1 2.5 %copy.55 = f32[4,256,256]{2,1,0:T(8,128)} copy(f32[4,256,256]{1,2,0:T(8,128)} %bitcast.36) | data formatting | bytes 2097152 | tf_op jit(solution)/shard_map/mul | solution.py:18
  41.7 2.6 %copy.49 = f32[4,256,256]{2,1,0:T(8,128)} copy(f32[4,256,256]{1,2,0:T(8,128)} %bitcast.37) | data formatting | bytes 2097152 | tf_op jit(solution)/shard_map/mul | solution.py:18
  44.2 20.6 %all-gather.bm_ref = f32[16,1,256]{2,1,0:T(1,128)} all-gather(f32[1,1,256]{2,1,0:T(1,128)S(1)} %bitcast.44), channel_id=1, replica_groups=mesh['group'=2,'gx'=16] {'gx'}, dimensions={0}, use_global_device_ids=true | all-gather | bytes 17408 | tf_op jit(solution)/shard_map/all_gather | solution.py:119
  64.9 18.3 %all-gather.1.bo_ref = f32[16,1,256]{2,1,0:T(1,128)} all-gather(f32[1,1,256]{2,1,0:T(1,128)S(1)} %bitcast.45), channel_id=1, replica_groups=mesh['group'=2,'gx'=16] {'gx'}, dimensions={0}, use_global_device_ids=true | all-gather | bytes 17408 | tf_op jit(solution)/shard_map/all_gather | solution.py:121
  84.2 1.7 %copy.58 = f32[1,256,256]{1,2,0:T(8,128)} copy(bf16[1,256,256]{2,1,0:T(8,128)(2,1)} %collective-permute-done) | data formatting | bytes 393216 | tf_op jit(solution)/shard_map/convert_element_type | solution.py:146
  86.0 1.5 %multiply_subtract_fusion.1 = f32[4,256,4,64]{1,3,2,0:T(8,128)S(1)} fusion(f32[4,256,4,64]{1,3,2,0:T(8,128)S(1)} %bitcast.31, f32[1,256,4,64]{1,3,2,0:T(8,128)} %bitcast.42, f32[3,256,4,64]{1,3,2,0:T(8,128)} %bitcast.39, f32[4,256,64]{1,2,0:T(8,128)} %get-tuple-element.103, f32[4,256,64]{1,2,0:T(8,128)S(1)} %get-tuple-element.104), kind=kLoop, calls=%fused_computation.32 | loop fusion | flops 1572864 | bytes 3670016 | tf_op jit(solution)/shard_map/sub | solution.py:18
  88.6 1.2 fusion.18
  89.8 6.0 %collective-permute-done.1 = bf16[1,256,4,64]{1,3,2,0:T(8,128)(2,1)S(1)} collective-permute-done((bf16[1,256,4,64]{1,3,2,0:T(8,128)(2,1)S(1)}, bf16[1,256,4,64]{1,3,2,0:T(8,128)(2,1)S(1)}, u32[]{:S(2)}, u32[]{:S(2)}) %collective-permute-start.1) | collective-permute-done | bytes 131104 | tf_op jit(solution)/shard_map/ppermute | solution.py:13
  96.8 6.9 %fusion.5 = f32[1,4,256,256]{3,0,2,1:T(1,128)S(1)} fusion(bf16[3,3,256,256]{3,2,1,0:T(8,128)(2,1)S(1)} %bitcast.30, bf16[1,6,258,256]{3,2,1,0:T(8,128)(2,1)S(1)} %fusion.18), kind=kOutput, calls=%fused_computation.14 | convolution fusion | flops 1207959552 | bytes 3020800 | tf_op jit(solution)/shard_map/conv_general_dilated | solution.py:129
  106.4 1.1 multiply_convert_fusion.h1_ref
  107.5 1.2 copy.60
  108.8 1.6 %convert_element_type.57 = f32[1,256,256]{2,1,0:T(8,128)} convert(bf16[1,256,256]{2,1,0:T(8,128)(2,1)} %collective-permute-done) | non-fusion elementwise | flops 65536 | bytes 393216 | tf_op jit(solution)/shard_map/convert_element_type | solution.py:146
  111.2 2.4 %copy.61 = f32[3,256,256]{2,1,0:T(8,128)} copy(f32[3,256,256]{1,2,0:T(8,128)} %bitcast.34) | data formatting | bytes 1572864 | tf_op jit(solution)/shard_map/concatenate | solution.py:22
  114.4 1.2 copy.70
  117.4 16.3 %shard_map.100 = f32[4,256,256]{2,1,0:T(8,128)} custom-call(s32[23]{0:T(128)} %get-tuple-element.108.tile_ref, s32[23]{0:T(128)} %select_clamp_fusion.band_ref, s32[23]{0:T(128)} %fusion.23.valid_ref, bf16[4,256,256]{2,1,0:T(8,128)(2,1)} %multiply_convert_fusion.h1_ref, s32[256,1]{1,0:T(8,128)} %copy.72.bid_ref, ...), custom_call_target="tpu_custom_call" | custom-call | tf_op jit(solution)/shard_map/pallas_call | solution.py:82
  133.6 4.6 %fusion.12 = f32[4,256,256]{2,1,0:T(8,128)} fusion(f32[4,256,256]{2,1,0:T(8,128)} %shard_map.100, f32[4,256,256]{2,1,0:T(8,128)S(1)} %copy-done.1, f32[3,256,256]{2,1,0:T(8,128)} %copy.70, f32[1,256,256]{2,1,0:T(8,128)} %copy.69, f32[4,256,256]{2,1,0:T(8,128)} %copy.68, f32[4,256,256]{2,1,0:T(8,128)} %copy.49, f32[3,256,256]{2,1,0:T(8,128)} %copy.60, ...), kind=kLoop, calls=%fused_computation.28 | loop fusion | flops 5505024 | bytes 10485760 | tf_op jit(solution)/shard_map/add | solution.py:151
  (111 shorter events, 24.6 us)
Async XLA Ops:
  6.5 90.2 %copy-start = (bf16[2304,256]{1,0:T(8,128)(2,1)S(1)}, bf16[2304,256]{1,0:T(8,128)(2,1)}, u32[]{:S(2)}) copy-start(bf16[2304,256]{1,0:T(8,128)(2,1)} %param.16) | copy-start | bytes 3538948
  6.5 9.1 %copy-start.16 = (s32[256]{0:T(256)S(1)}, s32[256]{0:T(256)}, u32[]{:S(2)}) copy-start(s32[256]{0:T(256)} %param.15) | copy-start | bytes 3076
  6.5 10.1 %copy-start.14 = (s32[2,4,16384]{2,1,0:T(4,128)S(1)}, s32[2,4,16384]{2,1,0:T(4,128)}, u32[]{:S(2)}) copy-start(s32[2,4,16384]{2,1,0:T(4,128)} %param.14) | copy-start | bytes 1572868
  6.5 110.8 %all-gather.5.cloned.1.call-start = ((), (), s32[]{:S(2)}) async-start(), calls=%async_computation | async-start | bytes 2228224 | tf_op jit(solution)/shard_map/all_gather | solution.py:118
  7.3 110.1 %all-gather.7.cloned.1.call-start = ((), (), s32[]{:S(2)}) async-start(), calls=%async_computation.1 | async-start | bytes 2228224 | tf_op jit(solution)/shard_map/all_gather | solution.py:120
  10.1 77.8 %collective-permute-start.4 = (bf16[1,256,256]{2,1,0:T(8,128)(2,1)}, bf16[1,256,256]{2,1,0:T(8,128)(2,1)}, u32[]{:S(2)}, u32[]{:S(2)}) collective-permute-start(bf16[1,256,256]{2,1,0:T(8,128)(2,1)} %get-tuple-element.100), channel_id=1, source_target_pairs={{0,1},{1,2},{2,3},{3,4},{4,5},{5,6},{6,7},{7,8},{8,9},{9,10},{10,1... | collective-permute-start | bytes 393224 | tf_op jit(solution)/shard_map/ppermute | solution.py:13
  10.6 73.7 %collective-permute-start = (bf16[1,256,256]{2,1,0:T(8,128)(2,1)}, bf16[1,256,256]{2,1,0:T(8,128)(2,1)}, u32[]{:S(2)}, u32[]{:S(2)}) collective-permute-start(bf16[1,256,256]{2,1,0:T(8,128)(2,1)} %get-tuple-element.101), channel_id=1, source_target_pairs={{0,15},{1,0},{2,1},{3,2},{4,3},{5,4},{6,5},{7,6},{8,7},{9,8},{10,9... | collective-permute-start | bytes 393224 | tf_op jit(solution)/shard_map/ppermute | solution.py:13
  16.7 6.1 %copy-start.15 = (f32[4,16384]{1,0:T(4,128)S(1)}, f32[4,16384]{1,0:T(4,128)}, u32[]{:S(2)}) copy-start(f32[4,16384]{1,0:T(4,128)} %param.13) | copy-start | bytes 786436
  23.8 3.1 %copy-start.1 = (f32[4,256,256]{2,1,0:T(8,128)S(1)}, f32[4,256,256]{2,1,0:T(8,128)}, u32[]{:S(2)}) copy-start(f32[4,256,256]{2,1,0:T(8,128)} %param.12) | copy-start | bytes 3145732
  40.6 3.6 %copy-start.17 = (f32[1,256]{1,0:T(1,128)S(1)}, f32[1,256]{1,0:T(1,128)}, u32[]{:S(2)}) copy-start(f32[1,256]{1,0:T(1,128)} %param.19) | copy-start | bytes 3076
  40.6 24.3 %copy-start.18 = (f32[1,256]{1,0:T(1,128)S(1)}, f32[1,256]{1,0:T(1,128)}, u32[]{:S(2)}) copy-start(f32[1,256]{1,0:T(1,128)} %param.21) | copy-start | bytes 3076
  87.4 1.2 copy-start.8
  87.5 8.5 %copy-start.3 = (f32[3,256,4,64]{1,3,2,0:T(8,128)}, f32[3,256,4,64]{1,3,2,0:T(8,128)S(1)}, u32[]{:S(2)}) copy-start(f32[3,256,4,64]{1,3,2,0:T(8,128)S(1)} %slice.71) | copy-start | bytes 2359300
  87.5 8.2 %collective-permute-start.1 = (bf16[1,256,4,64]{1,3,2,0:T(8,128)(2,1)S(1)}, bf16[1,256,4,64]{1,3,2,0:T(8,128)(2,1)S(1)}, u32[]{:S(2)}, u32[]{:S(2)}) collective-permute-start(bf16[1,256,4,64]{1,3,2,0:T(8,128)(2,1)S(1)} %slice.84), channel_id=1, source_target_pairs={{0,1},{1,2},{2,3},{3,4},{4,5},{5,6},{6,7},{7,8},{8,9},{9,10},{10,1... | collective-permute-start | bytes 393224 | tf_op jit(solution)/shard_map/ppermute | solution.py:13
  96.5 7.3 %collective-permute-start.2 = (bf16[1,256,4,64]{1,3,2,0:T(8,128)(2,1)S(1)}, bf16[1,256,4,64]{1,3,2,0:T(8,128)(2,1)S(1)}, u32[]{:S(2)}, u32[]{:S(2)}) collective-permute-start(bf16[1,256,4,64]{1,3,2,0:T(8,128)(2,1)S(1)} %slice.83), channel_id=1, source_target_pairs={{0,15},{1,0},{2,1},{3,2},{4,3},{5,4},{6,5},{7,6},{8,7},{9,8},{10,9... | collective-permute-start | bytes 393224 | tf_op jit(solution)/shard_map/ppermute | solution.py:13
  103.8 1.1 copy-start.5
  104.6 1.8 %copy-start.19 = (f32[256]{0:T(256)S(1)}, f32[256]{0:T(256)}, u32[]{:S(2)}) copy-start(f32[256]{0:T(256)} %param.17) | copy-start | bytes 3076
  104.9 2.6 %copy-start.4 = (f32[3,256,4,64]{1,3,2,0:T(8,128)S(1)}, f32[3,256,4,64]{1,3,2,0:T(8,128)}, u32[]{:S(2)}) copy-start(f32[3,256,4,64]{1,3,2,0:T(8,128)} %copy-done.3) | copy-start | bytes 2359300
  105.9 4.5 %copy-start.11 = (f32[1,256,4,64]{1,3,2,0:T(8,128)S(1)}, f32[1,256,4,64]{1,3,2,0:T(8,128)}, u32[]{:S(2)}) copy-start(f32[1,256,4,64]{1,3,2,0:T(8,128)} %copy-done.10) | copy-start | bytes 786436
  105.9 9.7 %collective-permute-start.3 = (bf16[1,256,4,64]{1,3,2,0:T(8,128)(2,1)}, bf16[1,256,4,64]{1,3,2,0:T(8,128)(2,1)}, u32[]{:S(2)}, u32[]{:S(2)}) collective-permute-start(bf16[1,256,4,64]{1,3,2,0:T(8,128)(2,1)} %slice.82), channel_id=1, source_target_pairs={{0,1},{1,2},{2,3},{3,4},{4,5},{5,6},{6,7},{7,8},{8,9},{9,10},{10,1... | collective-permute-start | bytes 393224 | tf_op jit(solution)/shard_map/ppermute | solution.py:13
  111.2 3.2 %slice-start = ((f32[4,256,4,64]{1,3,2,0:T(8,128)}), f32[3,256,4,64]{1,3,2,0:T(8,128)S(1)}, s32[]{:S(2)}) async-start(f32[4,256,4,64]{1,3,2,0:T(8,128)} %copy-done.6), calls=%async_computation.2 | async-start | bytes 1572864 | tf_op jit(solution)/shard_map/slice | solution.py:25
  117.3 16.3 %copy-start.2 = (f32[3,256,256]{2,1,0:T(8,128)S(1)}, f32[3,256,256]{2,1,0:T(8,128)}, u32[]{:S(2)}) copy-start(f32[3,256,256]{2,1,0:T(8,128)} %slice.48) | copy-start | bytes 2359300
  117.3 16.3 %copy-start.12 = (f32[1,256,256]{2,1,0:T(8,128)S(1)}, f32[1,256,256]{2,1,0:T(8,128)}, u32[]{:S(2)}) copy-start(f32[1,256,256]{2,1,0:T(8,128)} %convert_element_type.57) | copy-start | bytes 786436
  117.4 16.3 %copy-start.13 = (f32[1,256,256]{2,1,0:T(8,128)S(1)}, f32[1,256,256]{2,1,0:T(8,128)}, u32[]{:S(2)}) copy-start(f32[1,256,256]{2,1,0:T(8,128)} %copy.59) | copy-start | bytes 786436
  (4 other events, 3.5 us)
Sparse Core Ops, SparseCore 0:
  9.5 44.1 all-gather.4
  55.9 40.1 all-gather.6

commit v2 on v1

v2 whole, which is shorter than its diff:
```python
import jax
import jax.numpy as jnp
from jax import lax
from jax.experimental import pallas as pl
from jax.experimental.pallas import tpu as pltpu
from jax.sharding import PartitionSpec as P

BIAS_ROWS = 16


def passed_along(array, axis, by):
    length = lax.axis_size(axis)
    return lax.ppermute(array, axis, [(i, (i + by) % length) for i in range(length)])


def split_three(values):
    high = values.astype(jnp.bfloat16)
    rest = values - high.astype(jnp.float32)
    middle = rest.astype(jnp.bfloat16)
    low = (rest - middle.astype(jnp.float32)).astype(jnp.bfloat16)
    return [high, middle, low]


def pack_band(weight_mid, bias_mid, weight_out, bias_out):
    hidden = weight_mid.shape[-1]
    rows = split_three(bias_mid[0]) + split_three(bias_out[0])
    rows = jnp.stack(rows, 0)
    rows = jnp.pad(rows, ((0, BIAS_ROWS - rows.shape[0]), (0, 0)))
    return jnp.concatenate([weight_mid[0], weight_out[0], rows], 0)[None]


def face_flux(left_vals, right_vals, speeds, switch_now):
    damping = switch_now * speeds * speeds + (1.0 - switch_now) * jnp.abs(speeds)
    return 0.5 * speeds * (left_vals + right_vals) - 0.5 * damping * (right_vals - left_vals)


def flux_change(values, right_col, speeds, switch_now):
    right_vals = jnp.concatenate([values[1:], right_col], 0)
    edge_flux = face_flux(values, right_vals, speeds, switch_now)
    left_flux = passed_along(edge_flux[-1:].astype(jnp.bfloat16), "gx", 1).astype(jnp.float32)
    return edge_flux - jnp.concatenate([left_flux, edge_flux[:-1]], 0)


def band_kernel(tile_ref, slot_ref, band_ref, valid_ref, h1_ref, bid_ref, wm_ref, wo_ref, b_ref, out_ref):
    step = pl.program_id(0)
    band = band_ref[step]
    first = jnp.logical_or(step == 0, tile_ref[step] != tile_ref[jnp.maximum(step - 1, 0)])

    @pl.when(first)
    def _():
        out_ref[...] = jnp.zeros_like(out_ref)

    @pl.when(valid_ref[step] == 1)
    def _():
        lon, rows, hidden = h1_ref.shape
        parts = b_ref[0].astype(jnp.float32)
        bias_mid = (parts[0:1] + parts[1:2]) + parts[2:3]
        bias_out = (parts[3:4] + parts[4:5]) + parts[5:6]
        block = h1_ref[...].reshape(lon * rows, hidden)
        middle = jnp.dot(block, wm_ref[0], preferred_element_type=jnp.float32) + bias_mid
        hidden_two = (middle / (1.0 + jnp.exp(-middle))).astype(jnp.bfloat16)
        result = jnp.dot(hidden_two, wo_ref[0], preferred_element_type=jnp.float32) + bias_out
        result = result.astype(jnp.bfloat16).astype(jnp.float32)
        result = result.reshape(lon, rows, result.shape[-1])
        mask = (bid_ref[...] == band)[None]
        out_ref[...] = jnp.where(mask, result, out_ref[...])


def band_networks(hidden_one, strip_table, packed, tile_rows):
    lon, lat_rows, hidden = hidden_one.shape
    channels = packed.shape[-1]
    bands = packed.shape[0]
    me = lax.axis_index("gx")
    tiles = lat_rows // tile_rows
    steps = tiles + bands - 1
    low = strip_table[0::tile_rows]
    high = strip_table[tile_rows - 1 :: tile_rows]
    count = high - low + 1
    offset = jnp.cumsum(count) - count
    total = jnp.sum(count)
    index = jnp.arange(steps, dtype=jnp.int32)
    started = (offset[None, :] <= index[:, None]).astype(jnp.int32)
    tile = jnp.clip(jnp.sum(started, 1) - 1, 0, tiles - 1)
    pick = (tile[:, None] == jnp.arange(tiles, dtype=jnp.int32)[None, :]).astype(jnp.int32)
    band = jnp.sum(pick * low[None, :], 1) + index - jnp.sum(pick * offset[None, :], 1)
    valid = index < total
    tile = jnp.where(valid, tile, tiles - 1).astype(jnp.int32)
    band = jnp.clip(jnp.where(valid, band, high[tiles - 1]), 0, bands - 1).astype(jnp.int32)
    slot = band
    valid = valid.astype(jnp.int32)
    band_ids = strip_table.reshape(lat_rows, 1)
    del me
    grid_spec = pltpu.PrefetchScalarGridSpec(
        num_scalar_prefetch=4,
        grid=(steps,),
        in_specs=[
            pl.BlockSpec((lon, tile_rows, hidden), lambda s, t, k, b, v: (0, t[s], 0)),
            pl.BlockSpec((tile_rows, 1), lambda s, t, k, b, v: (t[s], 0)),
            pl.BlockSpec((1, hidden, hidden), lambda s, t, k, b, v: (k[s], 0, 0)),
            pl.BlockSpec((1, hidden, channels), lambda s, t, k, b, v: (k[s], 1, 0)),
            pl.BlockSpec((1, BIAS_ROWS, channels), lambda s, t, k, b, v: (k[s], 2 * hidden // BIAS_ROWS, 0)),
        ],
        out_specs=pl.BlockSpec((lon, tile_rows, channels), lambda s, t, k, b, v: (0, t[s], 0)),
    )
    return pl.pallas_call(
        band_kernel,
        grid_spec=grid_spec,
        out_shape=jax.ShapeDtypeStruct((lon, lat_rows, channels), jnp.float32),
        compiler_params=pltpu.CompilerParams(dimension_semantics=("arbitrary",)),
    )(tile, slot, band, valid, hidden_one, band_ids, packed, packed, packed)


def widened(values, field_count):
    lon, rows, levels = values.shape
    return jnp.broadcast_to(values[:, :, None, :], (lon, rows, field_count, levels)).reshape(
        lon, rows, field_count * levels
    )


def on_device(
    fields,
    courant,
    switches,
    strip_table,
    weight_in,
    bias_in,
    weight_mid,
    bias_mid,
    weight_out,
    bias_out,
):
    lon_dev, lat_rows, channels = fields.shape
    levels = courant.shape[1] // lat_rows
    field_count = channels // levels
    hidden = weight_in.shape[1]
    tile_rows = min(32, lat_rows)

    packed = pack_band(weight_mid, bias_mid, weight_out, bias_out)
    packed = lax.all_gather(packed, "gx", axis=0, tiled=True)

    columns_bf = fields.astype(jnp.bfloat16)
    west_col = passed_along(columns_bf[-1:], "gx", 1)
    east_col = passed_along(columns_bf[:1], "gx", -1)
    padded = jnp.concatenate([west_col, columns_bf, east_col], 0)
    padded = jnp.pad(padded, ((0, 0), (1, 1), (0, 0)))
    kernel = weight_in.reshape(3, 3, channels, hidden)
    summed = lax.conv_general_dilated(
        padded[None],
        kernel,
        (1, 1),
        "VALID",
        dimension_numbers=("NHWC", "HWIO", "NHWC"),
        preferred_element_type=jnp.float32,
    )[0]
    summed = summed + bias_in
    hidden_one = jax.nn.silu(summed).astype(jnp.bfloat16)

    tendency = band_networks(hidden_one, strip_table, packed, tile_rows)

    speeds = widened(courant.reshape(lon_dev, lat_rows, levels), field_count)
    switch_one = widened(switches[0].reshape(lon_dev, lat_rows, levels).astype(jnp.float32), field_count)
    switch_two = widened(switches[1].reshape(lon_dev, lat_rows, levels).astype(jnp.float32), field_count)
    ahead_col = east_col.astype(jnp.float32)
    section_one = fields - flux_change(fields, ahead_col, speeds, switch_one)
    ahead_two = passed_along(section_one[:1].astype(jnp.bfloat16), "gx", -1).astype(jnp.float32)
    section_two = section_one - flux_change(section_one, ahead_two, speeds, switch_two)
    moved = 0.5 * fields + 0.5 * section_two
    return moved + tendency


def solution(mesh):
    return jax.shard_map(
        on_device,
        mesh=mesh,
        in_specs=(
            P(("group", "gx"), None, None),
            P(("group", "gx"), None),
            P(None, ("group", "gx"), None),
            P("group"),
            P(),
            P(),
            P("gx", None, None),
            P("gx", None),
            P("gx", None, None),
            P("gx", None),
        ),
        out_specs=P(("group", "gx"), None, None),
        check_vma=False,
    )
```

time: 147 us -> 93.7 us (0.64)
  blocking collectives: 38.9 us -> 0 us
  local copies, waits for them, and re-layouts: 37.3 us -> 13.3 us
  waiting for transfers between devices: 6.75 us -> 17.1 us
    all_gather x2 -> x0, blocking collectives: 38.9 us -> none  [the longest x1 20.6 us: on_device(): all_bmid = lax.all_gather(bias_mid, 'gx', axis=0, tiled=True)]
    mul x6 -> x0, local copies, waits for them, and re-layouts: 12.8 us -> none  [the longest x4 9.16 us: face_flux(): 0.5 * damping * (right_vals - left_vals)]
    concatenate x6 -> x0, local copies, waits for them, and re-layouts: 7.27 us -> none  [the longest x4 4.08 us: flux_change(): return edge_flux - jnp.concatenate([left_flux, edge_flux[:-1]], 0)]
    ppermute x5, waiting for transfers between devices: 6.02 us -> 11.9 us  [passed_along(): lax.ppermute(array, axis, [(i, (i + by) % length) for i in range(length)])]
    all_gather x2 -> x1, waiting for transfers between devices: 0.01 us -> 5.27 us  [on_device(): packed = lax.all_gather(packed, 'gx', axis=0, tiled=True)]
    reshape x2 -> x3, local copies, waits for them, and re-layouts: 0.48 us -> 5.17 us  [widened(): jnp.broadcast_to(values[:, :, None, :], (lon, rows, field_count, levels))]
    gather x6 -> x0, local copies, waits for them, and re-layouts: 4.19 us -> none  [the longest x4 2.79 us: band_networks(): jnp.searchsorted(offset, index, side='right').astype(jnp.int32) - 1]
    slice x3, local copies, waits for them, and re-layouts: 3.46 us -> 0.06 us  [flux_change(): right_vals = jnp.concatenate([values[1:], right_col], 0)]
  transfers between devices with their start and end apart: 7 -> 6, of which waited for: 1 -> 3; matrix products, arithmetic and copies ran while one was open for 38% -> 34% of each run, Pallas kernels for 0% -> 0%
where the time goes in v2:
time: 93.7 us; the launch traced here: 92.6 us
  other arithmetic  17.9 us (19%)
  Pallas kernels  17.6 us (19%)
  waiting for transfers between devices  17.1 us (18%)
  between operations  13.7 us (15%)
  local copies, waits for them, and re-layouts  13.3 us (14%)
  matrix products  6.89 us (7%)
  starting transfers between devices  6.13 us (7%)
    pallas_call x1, Pallas kernels, band_networks(): pl.pallas_call(band_kernel, grid_spec=grid_spec, out_shape=jax.ShapeDtype...  17.6 us
    ppermute x5, waiting for transfers between devices, passed_along(): lax.ppermute(array, axis, [(i, (i + by) % length) for i in range(length)])  11.9 us
    conv_general_dilated x1, matrix products, on_device(): lax.conv_general_dilated(padded[None], kernel, (1, 1), 'VALID', dimension...  6.89 us
    ppermute x5, starting transfers between devices, passed_along(): lax.ppermute(array, axis, [(i, (i + by) % length) for i in range(length)])  6.12 us
    all_gather x1, waiting for transfers between devices, on_device(): packed = lax.all_gather(packed, 'gx', axis=0, tiled=True)  5.27 us
    reshape x3, local copies, waits for them, and re-layouts, widened(): jnp.broadcast_to(values[:, :, None, :], (lon, rows, field_count, levels))  5.17 us
    add x1, other arithmetic, on_device(): return moved + tendency  3.16 us
    broadcast_in_dim x5, local copies, waits for them, and re-layouts, widened(): jnp.broadcast_to(values[:, :, None, :], (lon, rows, field_count, levels))  2.84 us
  transfers between devices with their start and end apart: 6, of which 3 were waited for; matrix products, arithmetic and copies ran while one was open for 34% of the time, Pallas kernels for 0%

profile of v2, /device:TPU:0, one launch (start us, length us, event | category | flops | bytes accessed | tf_op | source)
XLA Modules:
  0.0 92.6 jit_solution(15359404435876898550)
XLA Ops:
  6.5 0.9 subtract_convert_fusion
  7.4 1.7 %fusion.23 = bf16[528,256]{1,0:T(8,128)(2,1)} fusion(bf16[6,256]{1,0:T(8,128)(2,1)S(1)} %stack.2, bf16[256,256]{1,0:T(8,128)(2,1)} %bitcast.27, bf16[256,256]{1,0:T(8,128)(2,1)} %bitcast.28), kind=kLoop, calls=%fused_computation.34 | loop fusion | flops 1081344 | bytes 535552 | tf_op jit(solution)/shard_map/concatenate | solution.py:29
  9.1 1.3 %convert_element_type.100 = bf16[4,256,256]{2,1,0:T(8,128)(2,1)S(1)} convert(f32[4,256,256]{2,1,0:T(8,128)} %param.10) | non-fusion elementwise | flops 262144 | bytes 1572864 | tf_op jit(solution)/shard_map/convert_element_type | solution.py:141
  11.2 5.5 %collective-permute-start = (bf16[1,256,256]{2,1,0:T(8,128)(2,1)}, bf16[1,256,256]{2,1,0:T(8,128)(2,1)}, u32[]{:S(2)}, u32[]{:S(2)}) collective-permute-start(bf16[1,256,256]{2,1,0:T(8,128)(2,1)} %get-tuple-element.10), channel_id=1, source_target_pairs={{0,15},{1,0},{2,1},{3,2},{4,3},{5,4},{6,5},{7,6},{8,7},{9,8},{10,9... | collective-permute-start | bytes 393224 | tf_op jit(solution)/shard_map/ppermute | solution.py:13
  18.3 1.1 %add_clamp_fusion = (s32[23]{0:T(128)S(1)}, s32[23]{0:T(128)}) fusion(s32[23]{0:T(128)S(1)} %convert_reduce_fusion, s32[]{:T(128)} %get-tuple-element.18), kind=kLoop, calls=%fused_computation.51 | loop fusion | flops 92 | bytes 280 | tf_op jit(solution)/shard_map/jit(clip)/min | solution.py:83
  19.6 1.7 %select_clamp_fusion.slot_ref.band_ref = s32[23]{0:T(128)} fusion(s32[23]{0:T(128)S(1)} %get-tuple-element.6, s32[23]{0:T(128)S(1)} %get-tuple-element.5, s32[]{:T(128)} %bitcast.5, s32[]{:T(128)} %get-tuple-element.18), kind=kLoop, calls=%fused_computation.50 | loop fusion | flops 115 | bytes 284 | tf_op jit(solution)/shard_map/jit(clip)/min | solution.py:88
  21.3 0.8 copy.41.bid_ref
  22.7 1.3 %copy.28 = f32[4,256,256]{2,1,0:T(8,128)} copy(f32[4,256,256]{1,2,0:T(8,128)S(1)} %bitcast.24) | data formatting | bytes 2097152 | tf_op jit(solution)/shard_map/reshape | solution.py:115
  24.6 1.3 %copy.30 = f32[4,256,256]{2,1,0:T(8,128)} copy(f32[4,256,256]{1,2,0:T(8,128)S(1)} %bitcast.25) | data formatting | bytes 2097152 | tf_op jit(solution)/shard_map/reshape | solution.py:115
  26.2 0.9 copy.35
  27.1 2.2 %broadcast_in_dim.21 = f32[4,256,4,64]{1,3,2,0:T(8,128)} broadcast(f32[4,256,64]{1,2,0:T(8,128)} %copy.35), dimensions={0,1,3} | broadcast | bytes 1310720 | tf_op jit(solution)/shard_map/broadcast_in_dim | solution.py:115
  29.3 2.6 %copy.36 = f32[4,256,256]{2,1,0:T(8,128)} copy(f32[4,256,256]{1,2,0:T(8,128)} %bitcast.26) | data formatting | bytes 2097152 | tf_op jit(solution)/shard_map/reshape | solution.py:115
  31.9 1.1 %fusion.24.valid_ref = s32[23]{0:T(128)} fusion(s32[]{:T(128)} %get-tuple-element.18), kind=kLoop, calls=%fused_computation.54 | loop fusion | flops 46 | bytes 96 | tf_op jit(solution)/shard_map/convert_element_type | solution.py:90
  33.0 0.9 convert_element_type.101
  33.9 2.0 %fusion.6 = f32[4,256,256]{2,1,0:T(8,128)S(1)} fusion(f32[4,256,256]{2,1,0:T(8,128)} %copy.28, f32[4,256,256]{2,1,0:T(8,128)} %copy.30, f32[4,256,256]{2,1,0:T(8,128)S(1)} %copy-done.1, f32[1,256,256]{2,1,0:T(8,128)S(1)} %convert_element_type.101, f32[3,256,256]{2,1,0:T(8,128)S(1)} %slice-done), kind=kLoop, calls=%fused_computation.10 | loop fusion | flops 3670016 | bytes 5242880 | tf_op jit(solution)/shard_map/sub | solution.py:34
  36.1 1.2 %fusion.21 = bf16[1,6,258,256]{3,2,1,0:T(8,128)(2,1)S(1)} fusion(bf16[1,256,256]{2,1,0:T(8,128)(2,1)} %collective-permute-done, bf16[4,256,256]{2,1,0:T(8,128)(2,1)S(1)} %convert_element_type.100, bf16[1,256,256]{2,1,0:T(8,128)(2,1)} %collective-permute-done.4), kind=kLoop, calls=%fused_computation.31 | loop fusion | flops 4755456 | bytes 1579008 | tf_op jit(solution)/shard_map/broadcast_in_dim | solution.py:148
  37.2 6.0 %collective-permute-done.1 = bf16[1,256,256]{2,1,0:T(8,128)(2,1)S(1)} collective-permute-done((bf16[1,256,256]{2,1,0:T(8,128)(2,1)S(1)}, bf16[1,256,256]{2,1,0:T(8,128)(2,1)S(1)}, u32[]{:S(2)}, u32[]{:S(2)}) %collective-permute-start.1) | collective-permute-done | bytes 131104 | tf_op jit(solution)/shard_map/ppermute | solution.py:13
  43.6 6.9 %fusion.1 = f32[1,4,256,256]{3,0,2,1:T(1,128)S(1)} fusion(bf16[3,3,256,256]{3,2,1,0:T(8,128)(2,1)S(1)} %bitcast.20, bf16[1,6,258,256]{3,2,1,0:T(8,128)(2,1)S(1)} %fusion.21), kind=kOutput, calls=%fused_computation.3 | convolution fusion | flops 1207959552 | bytes 3020800 | tf_op jit(solution)/shard_map/conv_general_dilated | solution.py:147
  50.6 1.1 %copy-done.3 = f32[4,256,256]{2,1,0:T(8,128)S(1)} copy-done((f32[4,256,256]{2,1,0:T(8,128)S(1)}, f32[4,256,256]{2,1,0:T(8,128)}, u32[]{:S(2)}) %copy-start.3) | copy-done | bytes 1048600
  52.7 1.1 %multiply_convert_fusion.h1_ref = bf16[4,256,256]{2,1,0:T(8,128)(2,1)} fusion(f32[1,4,256,256]{3,0,2,1:T(1,128)S(1)} %fusion.1, f32[256]{0:T(256)S(1)} %copy-done.9), kind=kLoop, calls=%fused_computation.25 | loop fusion | flops 1572864 | bytes 1573888 | tf_op jit(solution)/shard_map/convert_element_type | solution.py:156
  53.8 5.9 %collective-permute-done.3 = bf16[1,256,256]{2,1,0:T(8,128)(2,1)S(1)} collective-permute-done((bf16[1,256,256]{2,1,0:T(8,128)(2,1)S(1)}, bf16[1,256,256]{2,1,0:T(8,128)(2,1)S(1)}, u32[]{:S(2)}, u32[]{:S(2)}) %collective-permute-start.3) | collective-permute-done | bytes 131104 | tf_op jit(solution)/shard_map/ppermute | solution.py:13
  59.7 5.3 %all-gather.3.cloned.1.call-done = bf16[8448,256]{1,0:T(8,128)(2,1)} async-done(((bf16[528,256]{1,0:T(8,128)(2,1)}), bf16[8448,256]{1,0:T(8,128)(2,1)}) %all-gather.3.cloned.1.call-update) | async-done | bytes 4325392 | tf_op jit(solution)/shard_map/all_gather | solution.py:139
  65.0 17.6 %shard_map.100 = f32[4,256,256]{2,1,0:T(8,128)} custom-call(s32[23]{0:T(128)} %get-tuple-element.20.tile_ref, s32[23]{0:T(128)} %select_clamp_fusion.slot_ref.band_ref, s32[23]{0:T(128)} %select_clamp_fusion.slot_ref.band_ref, s32[23]{0:T(128)} %fusion.24.valid_ref, bf16[4,256,256]{2,1,0:T(8,128)(2,1)} %multiply_convert_fusion.h1_ref, ...), custom_call_target="tpu_custom_call" | custom-call | tf_op jit(solution)/shard_map/pallas_call | solution.py:105
  82.6 3.2 %fusion.15 = f32[4,256,256]{2,1,0:T(8,128)} fusion(f32[4,256,256]{2,1,0:T(8,128)} %shard_map.100, f32[4,256,256]{2,1,0:T(8,128)S(1)} %copy-done.1, f32[4,256,256]{2,1,0:T(8,128)} %copy-done.2, f32[4,256,256]{2,1,0:T(8,128)} %copy-done.4, f32[3,256,256]{2,1,0:T(8,128)S(1)} %slice-done.1, f32[1,256,256]{2,1,0:T(8,128)S(1)} %convert_element_type.108), kind=kLoop, calls=%fused_computation.23 | loop fusion | flops 1572864 | bytes 6291456 | tf_op jit(solution)/shard_map/add | solution.py:168
  (60 shorter events, 5.6 us)
Async XLA Ops:
  6.5 37.0 %copy-start = (bf16[2304,256]{1,0:T(8,128)(2,1)S(1)}, bf16[2304,256]{1,0:T(8,128)(2,1)}, u32[]{:S(2)}) copy-start(bf16[2304,256]{1,0:T(8,128)(2,1)} %param.14) | copy-start | bytes 3538948
  6.5 10.1 %copy-start.8 = (s32[256]{0:T(256)S(1)}, s32[256]{0:T(256)}, u32[]{:S(2)}) copy-start(s32[256]{0:T(256)} %param.13) | copy-start | bytes 3076
  6.5 12.9 %copy-start.6 = (s32[2,4,16384]{2,1,0:T(4,128)S(1)}, s32[2,4,16384]{2,1,0:T(4,128)}, u32[]{:S(2)}) copy-start(s32[2,4,16384]{2,1,0:T(4,128)} %param.12) | copy-start | bytes 1572868
  6.5 58.4 %all-gather.3.cloned.1.call-start = ((), (), s32[]{:S(2)}) async-start(), calls=%async_computation | async-start | bytes 4595712 | tf_op jit(solution)/shard_map/all_gather | solution.py:139
  10.4 11.7 %copy-start.7 = (f32[4,16384]{1,0:T(4,128)S(1)}, f32[4,16384]{1,0:T(4,128)}, u32[]{:S(2)}) copy-start(f32[4,16384]{1,0:T(4,128)} %param.11) | copy-start | bytes 786436
  11.2 21.8 %collective-permute-start = (bf16[1,256,256]{2,1,0:T(8,128)(2,1)}, bf16[1,256,256]{2,1,0:T(8,128)(2,1)}, u32[]{:S(2)}, u32[]{:S(2)}) collective-permute-start(bf16[1,256,256]{2,1,0:T(8,128)(2,1)} %get-tuple-element.10), channel_id=1, source_target_pairs={{0,15},{1,0},{2,1},{3,2},{4,3},{5,4},{6,5},{7,6},{8,7},{9,8},{10,9... | collective-permute-start | bytes 393224 | tf_op jit(solution)/shard_map/ppermute | solution.py:13
  16.6 19.4 %collective-permute-start.4 = (bf16[1,256,256]{2,1,0:T(8,128)(2,1)}, bf16[1,256,256]{2,1,0:T(8,128)(2,1)}, u32[]{:S(2)}, u32[]{:S(2)}) collective-permute-start(bf16[1,256,256]{2,1,0:T(8,128)(2,1)} %get-tuple-element.9), channel_id=1, source_target_pairs={{0,1},{1,2},{2,3},{3,4},{4,5},{5,6},{6,7},{7,8},{8,9},{9,10},{10,1... | collective-permute-start | bytes 393224 | tf_op jit(solution)/shard_map/ppermute | solution.py:13
  27.1 6.8 %copy-start.1 = (f32[4,256,256]{2,1,0:T(8,128)S(1)}, f32[4,256,256]{2,1,0:T(8,128)}, u32[]{:S(2)}) copy-start(f32[4,256,256]{2,1,0:T(8,128)} %param.10) | copy-start | bytes 3145732
  27.1 6.8 %slice-start = ((f32[4,256,256]{2,1,0:T(8,128)}), f32[3,256,256]{2,1,0:T(8,128)S(1)}, s32[]{:S(2)}) async-start(f32[4,256,256]{2,1,0:T(8,128)} %param.10), calls=%async_computation.1 | async-start | bytes 1572864 | tf_op jit(solution)/shard_map/slice | solution.py:38
  36.0 7.2 %collective-permute-start.1 = (bf16[1,256,256]{2,1,0:T(8,128)(2,1)S(1)}, bf16[1,256,256]{2,1,0:T(8,128)(2,1)S(1)}, u32[]{:S(2)}, u32[]{:S(2)}) collective-permute-start(bf16[1,256,256]{2,1,0:T(8,128)(2,1)S(1)} %slice.74), channel_id=1, source_target_pairs={{0,1},{1,2},{2,3},{3,4},{4,5},{5,6},{6,7},{7,8},{8,9},{9,10},{10,1... | collective-permute-start | bytes 393224 | tf_op jit(solution)/shard_map/ppermute | solution.py:13
  43.5 7.1 %copy-start.2 = (f32[4,256,256]{2,1,0:T(8,128)}, f32[4,256,256]{2,1,0:T(8,128)S(1)}, u32[]{:S(2)}) copy-start(f32[4,256,256]{2,1,0:T(8,128)S(1)} %fusion.11) | copy-start | bytes 3145732
  43.5 7.1 %collective-permute-start.2 = (bf16[1,256,256]{2,1,0:T(8,128)(2,1)S(1)}, bf16[1,256,256]{2,1,0:T(8,128)(2,1)S(1)}, u32[]{:S(2)}, u32[]{:S(2)}) collective-permute-start(bf16[1,256,256]{2,1,0:T(8,128)(2,1)S(1)} %slice.73), channel_id=1, source_target_pairs={{0,15},{1,0},{2,1},{3,2},{4,3},{5,4},{6,5},{7,6},{8,7},{9,8},{10,9... | collective-permute-start | bytes 393224 | tf_op jit(solution)/shard_map/ppermute | solution.py:13
  43.6 7.0 %copy-start.5 = (f32[4,256,256]{2,1,0:T(8,128)S(1)}, f32[4,256,256]{2,1,0:T(8,128)}, u32[]{:S(2)}) copy-start(f32[4,256,256]{2,1,0:T(8,128)} %copy.36) | copy-start | bytes 3145732
  50.5 1.2 %copy-start.3 = (f32[4,256,256]{2,1,0:T(8,128)S(1)}, f32[4,256,256]{2,1,0:T(8,128)}, u32[]{:S(2)}) copy-start(f32[4,256,256]{2,1,0:T(8,128)} %copy.28) | copy-start | bytes 3145732
  51.7 1.0 %copy-start.9 = (f32[256]{0:T(256)S(1)}, f32[256]{0:T(256)}, u32[]{:S(2)}) copy-start(f32[256]{0:T(256)} %param.15) | copy-start | bytes 3076
  52.2 1.7 %copy-start.4 = (f32[4,256,256]{2,1,0:T(8,128)}, f32[4,256,256]{2,1,0:T(8,128)S(1)}, u32[]{:S(2)}) copy-start(f32[4,256,256]{2,1,0:T(8,128)S(1)} %fusion.10) | copy-start | bytes 3145732
  52.2 7.5 %collective-permute-start.3 = (bf16[1,256,256]{2,1,0:T(8,128)(2,1)S(1)}, bf16[1,256,256]{2,1,0:T(8,128)(2,1)S(1)}, u32[]{:S(2)}, u32[]{:S(2)}) collective-permute-start(bf16[1,256,256]{2,1,0:T(8,128)(2,1)S(1)} %slice.72), channel_id=1, source_target_pairs={{0,1},{1,2},{2,3},{3,4},{4,5},{5,6},{6,7},{7,8},{8,9},{9,10},{10,1... | collective-permute-start | bytes 393224 | tf_op jit(solution)/shard_map/ppermute | solution.py:13
  65.0 17.6 %slice-start.1 = ((f32[4,256,256]{2,1,0:T(8,128)}), f32[3,256,256]{2,1,0:T(8,128)S(1)}, s32[]{:S(2)}) async-start(f32[4,256,256]{2,1,0:T(8,128)} %copy-done.4), calls=%async_computation.2 | async-start | bytes 1572864 | tf_op jit(solution)/shard_map/slice | solution.py:41
Sparse Core Ops, SparseCore 0:
  9.6 55.2 all-gather.2
